TPU v7x, 256 devices: a whole 4x4x8 slice. The times are simulated.
256 devices in a mesh: dp: 32 (over y, z), mp: 8 (over x, core).
Axes of the slice: x: 4, y: 4, z: 8, core: 2. Of those that a mesh axis runs over, the one named last changes fastest.
Arguments:
- hidden: bfloat16 [512, 32, 1024], P(('dp', 'mp')), may hold values from -96 to 96, as said below
- query_weight: bfloat16 [1024, 1024], P('dp', 'mp'), may hold values from -0.1875 to 0.1875
- w_key: bfloat16 [1024, 1024], P('dp', 'mp'), may hold values from -0.1875 to 0.1875
- w_value: bfloat16 [1024, 1024], P('dp', 'mp'), may hold values from -0.1875 to 0.1875
- rel_table: bfloat16 [512, 1024], P('dp'), may hold values from -6 to 6
- rel_bucket: int32 [32, 32], replicated, may hold values from 0 to 511
- w_out: bfloat16 [1024, 1024], P('mp', 'dp'), may hold values from -0.1875 to 0.1875
- w_up: bfloat16 [1024, 4096], P('dp', 'mp'), may hold values from -0.1875 to 0.1875
- w_down: bfloat16 [4096, 1024], P('mp', 'dp'), may hold values from -0.09375 to 0.09375
- w_proj: bfloat16 [1024, 128], P(('dp', 'mp')), may hold values from -0.1875 to 0.1875
- pages: bfloat16 [8192, 128, 128], P('dp'), may hold values from -0.59765625 to 0.59765625
- page_len: int32 [8192], P('dp'), may hold values from 1 to 128
- slot_per_page: int32 [8192], replicated, may hold values from 0 to 8191, as said below
- candidates: int32 [512, 16, 4], P(('dp', 'mp')), may hold values from 0 to 8191, as said below
Outputs:
- query_vectors: bfloat16 [512, 32, 128], P(('dp', 'mp'))
- scores: float32 [512, 16], P(('dp', 'mp'))
Inputs may be any that keep to these rules, and one draw needn't show every extreme that they name: slot_per_page is a permutation of the slots; the page in slot s is held by index s // 256 of dp. `candidates`: among the 128 page ids of the 2 queries of one device (queries in aligned blocks of 2), at most 8 have slots held by any one index of dp, and in every such block some index of dp holds exactly 8 of them. `hidden`: token states are finite.
All inputs are finite; a program needn't handle non-finite values.
Results may differ from a plain program's by a relative error of at most 0.025.
Values may be sent and summed in bfloat16 or wider, within the bound.
No kernel may reach another device: no remote copies, remote signals or barrier semaphores. Data moves between devices by JAX's collectives and lax.ppermute only.
A program may use at most 64 MiB of HBM per device.

v0:
```python
import jax
import jax.numpy as jnp
from jax import lax
from jax.sharding import PartitionSpec as P

HD = 64


def layer_norm(value):
    mean = jnp.mean(value, axis=-1, keepdims=True)
    centered = value - mean
    var = jnp.mean(centered * centered, axis=-1, keepdims=True)
    return centered / jnp.sqrt(var + 1e-07)


def add_rows(left, piece):
    return jnp.dot(left, piece, preferred_element_type=jnp.float32)


def return_maxima(maxima):
    return lax.all_to_all(
        maxima.astype(jnp.bfloat16), "dp", split_axis=0, concat_axis=0, tiled=True
    ).astype(maxima.dtype)


def body(
    hidden,
    query_weight,
    w_key,
    w_value,
    rel_table,
    rel_bucket,
    w_out,
    w_up,
    w_down,
    w_proj,
    pages,
    page_len,
    slot_per_page,
    candidates,
):
    qry_dev, qlen, width = hidden.shape
    heads_local = query_weight.shape[1] // HD
    cols = query_weight.shape[1]
    page_owners = lax.axis_size("dp")
    n_mp = lax.axis_size("mp")
    pg_dev = pages.shape[0]
    ptok = pages.shape[1]
    ncand, ppc = (candidates.shape[1], candidates.shape[2])
    req = qry_dev * ncand * ppc
    cap = 2 * req // page_owners
    slots = slot_per_page[candidates.reshape(req)]
    dest = slots // pg_dev
    local = slots % pg_dev
    query_of = jnp.arange(req, dtype=jnp.int32) // (ncand * ppc)
    member = (dest[:, None] == jnp.arange(page_owners, dtype=jnp.int32)[None, :]).astype(jnp.int32)
    place = jnp.sum((jnp.cumsum(member, axis=0) - 1) * member, axis=1)
    index = dest * cap + place
    codes = jnp.full((page_owners * cap,), -1, jnp.int32).at[index].set(query_of * pg_dev + local)
    codes = codes.reshape(page_owners, cap)
    got = lax.all_to_all(codes, "dp", split_axis=0, concat_axis=0, tiled=True)
    where_local = got % pg_dev
    which_query = jnp.clip(got // pg_dev, 0, qry_dev - 1)
    chosen = pages[where_local]
    lens = page_len[where_local]
    w_out_t = w_out.T
    w_down_t = w_down.T
    pieces = (query_weight, w_key, w_value, w_out_t, w_up, w_down_t, rel_table, w_proj)
    flat_pieces = jnp.concatenate([p.reshape(-1) for p in pieces])
    gathered = lax.all_gather(flat_pieces, "dp", axis=0, tiled=False)
    parts = []
    start = 0
    for p in pieces:
        size = p.size
        parts.append(gathered[:, start : start + size].reshape((page_owners,) + p.shape))
        start += size
    g_q, g_k, g_v, g_out, g_up, g_down, g_rel, g_proj = parts
    wq = g_q.reshape(page_owners * query_weight.shape[0], cols)
    wk = g_k.reshape(page_owners * w_key.shape[0], cols)
    wv = g_v.reshape(page_owners * w_value.shape[0], cols)
    wo = jnp.transpose(g_out, (2, 0, 1)).reshape(w_out.shape[0], page_owners * w_out.shape[1])
    wu = g_up.reshape(page_owners * w_up.shape[0], w_up.shape[1])
    wd = jnp.transpose(g_down, (2, 0, 1)).reshape(w_down.shape[0], page_owners * w_down.shape[1])
    left_rel = g_rel.reshape(page_owners * rel_table.shape[0], rel_table.shape[1])
    proj_all = lax.all_gather(g_proj, "mp", axis=0, tiled=False)
    wp = jnp.transpose(proj_all, (1, 0, 2, 3)).reshape(
        page_owners * n_mp * w_proj.shape[0], w_proj.shape[1]
    )
    tokens = lax.all_gather(hidden, "mp", axis=0, tiled=True)
    group = tokens.shape[0]
    flat = tokens.reshape(group * qlen, width)
    qsum = add_rows(flat, wq)
    ksum = add_rows(flat, wk)
    vsum = add_rows(flat, wv)
    qrsum = add_rows(left_rel, wq)
    krsum = add_rows(left_rel, wk)
    rel_q = qrsum.astype(jnp.bfloat16)
    rel_k = krsum.astype(jnp.bfloat16)
    nbuck = rel_q.shape[0]
    qx = qsum.astype(jnp.bfloat16).reshape(group, qlen, heads_local, HD)
    kx = ksum.astype(jnp.bfloat16).reshape(group, qlen, heads_local, HD)
    vx = vsum.astype(jnp.bfloat16).reshape(group, qlen, heads_local, HD)
    rel_q = rel_q.reshape(nbuck, heads_local, HD)
    rel_k = rel_k.reshape(nbuck, heads_local, HD)
    onehot = (rel_bucket[:, :, None] == jnp.arange(nbuck, dtype=jnp.int32)[None, None, :]).astype(
        jnp.float32
    )
    scale = 1.0 / jnp.sqrt(jnp.float32(3 * HD))
    content = jnp.einsum("qihd,qjhd->qhij", qx, kx, preferred_element_type=jnp.float32)
    along_axis_name = jnp.einsum("qihd,bhd->qhib", qx, rel_k, preferred_element_type=jnp.float32)
    c2p = jnp.einsum("qhib,ijb->qhij", along_axis_name, onehot, precision=lax.Precision.HIGHEST)
    back = jnp.einsum("qjhd,bhd->qhjb", kx, rel_q, preferred_element_type=jnp.float32)
    p2c = jnp.einsum("qhjb,jib->qhij", back, onehot, precision=lax.Precision.HIGHEST)
    logits = (content + c2p + p2c) * scale
    probs = jax.nn.softmax(logits, axis=-1).astype(jnp.bfloat16)
    context_rows = jnp.einsum("qhij,qjhd->qihd", probs, vx, preferred_element_type=jnp.float32)
    context_rows = context_rows.astype(jnp.bfloat16).reshape(group * qlen, cols)
    attn_terms = jnp.dot(context_rows, wo, preferred_element_type=jnp.float32)
    attn = lax.psum_scatter(
        attn_terms.astype(jnp.bfloat16), "mp", scatter_dimension=0, tiled=True
    ).astype(jnp.float32)
    own = hidden.reshape(qry_dev * qlen, width).astype(jnp.float32)
    mid = layer_norm(own + attn).astype(jnp.bfloat16)
    mid_all = lax.all_gather(mid, "mp", axis=0, tiled=True)
    up = add_rows(mid_all, wu)
    inner = jax.nn.gelu(up, approximate=False).astype(jnp.bfloat16)
    down_terms = jnp.dot(inner, wd, preferred_element_type=jnp.float32)
    mlp = lax.psum_scatter(
        down_terms.astype(jnp.bfloat16), "mp", scatter_dimension=0, tiled=True
    ).astype(jnp.float32)
    state = layer_norm(mid.astype(jnp.float32) + mlp).astype(jnp.bfloat16)
    width_out = w_proj.shape[1]
    proj = add_rows(state, wp)
    vectors = (proj / jnp.sqrt(jnp.sum(proj * proj, axis=-1, keepdims=True) + 1e-06)).astype(
        jnp.bfloat16
    )
    vectors = vectors.reshape(qry_dev, qlen, width_out)
    sent = jnp.broadcast_to(vectors[None], (page_owners, qry_dev, qlen, width_out))
    recv = lax.all_to_all(sent, "dp", split_axis=0, concat_axis=0, tiled=True)
    rows_in = jnp.take_along_axis(recv, which_query[:, :, None, None], axis=1)
    token_positions = jnp.arange(ptok, dtype=jnp.int32)
    sim = jnp.einsum("snie,snte->snit", rows_in, chosen, preferred_element_type=jnp.float32)
    valid = token_positions[None, None, None, :] < lens[:, :, None, None]
    returned = return_maxima(jnp.max(jnp.where(valid, sim, -1e30), axis=-1))
    best = returned.reshape(page_owners * cap, qlen)[index]
    best = best.reshape(qry_dev, ncand, ppc, qlen)
    scores = jnp.sum(jnp.max(best, axis=2), axis=-1)
    return (vectors, scores)


def solution(mesh):
    in_specs = (
        P(("dp", "mp"), None, None),
        P("dp", "mp"),
        P("dp", "mp"),
        P("dp", "mp"),
        P("dp", None),
        P(),
        P("mp", "dp"),
        P("dp", "mp"),
        P("mp", "dp"),
        P(("dp", "mp"), None),
        P("dp", None, None),
        P("dp"),
        P(),
        P(("dp", "mp"), None, None),
    )
    out_specs = (P(("dp", "mp"), None, None), P(("dp", "mp"), None))
    return jax.shard_map(body, mesh=mesh, in_specs=in_specs, out_specs=out_specs, check_vma=False)
```

profile of v0, /device:TPU:8, one launch (start us, length us, event | category | flops | bytes accessed | tf_op | source)
XLA Modules:
  0.0 330.8 jit_solution(3690136183016734294)
XLA Ops:
  7.2 0.7 bitcast_dynamic-update-slice_fusion.3
  7.9 0.8 copy.68
  8.7 0.8 copy.69
  9.5 0.8 copy.70
  10.2 0.7 bitcast_dynamic-update-slice_fusion.2
  10.9 0.7 bitcast_dynamic-update-slice_fusion.1
  11.6 0.7 bitcast_dynamic-update-slice_fusion
  12.4 0.7 constant_dynamic-update-slice_fusion
  13.0 0.8 reshape.444
  13.9 0.7 all-gather.6.cloned.1.call-update
  14.7 99.2 %all-gather.10.cloned.1.call-done = bf16[32,1,66048]{2,1,0:T(2,128)(2,1)} async-done(((bf16[1,1,66048]{2,1,0:T(2,128)(2,1)}), bf16[32,1,66048]{2,1,0:T(2,128)(2,1)}) %all-gather.10.cloned.1.call-update) | async-done | bytes 4227088 | tf_op jit(solution)/shard_map/all_gather | solution.py:70
  113.9 3.9 %copy.85 = bf16[32,1,66048]{2,0,1:T(8,128)(2,1)S(1)} copy(bf16[32,1,66048]{2,1,0:T(2,128)(2,1)} %all-gather.10.cloned.1.call-done) | data formatting | bytes 8454144
  117.8 1.5 fusion.123
  119.3 0.8 copy-done.2
  120.1 0.9 slice_bitcast_fusion
  121.1 1.6 reshape_reshape.18
  122.7 1.8 reshape_reshape.17
  124.5 1.1 convolution_convert_fusion.3
  125.6 2.1 convolution_convert_fusion.4
  127.7 12.2 %all-gather.6.cloned.1.call-done = bf16[16,32,1024]{2,1,0:T(8,128)(2,1)} async-done(((bf16[2,32,1024]{2,1,0:T(8,128)(2,1)}), bf16[16,32,1024]{2,1,0:T(8,128)(2,1)}) %all-gather.6.cloned.1.call-update) | async-done | bytes 1048592 | tf_op jit(solution)/shard_map/all_gather | solution.py:89
  139.9 1.8 fusion.17
  141.8 1.7 fusion.16
  144.1 0.5 fusion.63
  144.6 2.2 fusion.1
  146.7 0.5 fusion.65
  147.2 2.2 fusion.3
  149.4 2.2 copy.56
  151.7 1.7 fusion.13
  153.6 0.6 copy-done.8
  154.2 1.1 reshape_reshape.15
  155.3 1.1 fusion.15
  156.4 1.1 copy.50
  157.6 1.5 fusion.14
  159.2 0.2 copy.61
  159.6 1.4 convolution_convert_fusion
  161.1 34.7 %reduce-scatter.3.cloned.1.call-done = bf16[64,1024]{1,0:T(8,128)(2,1)} async-done(((bf16[512,1024]{1,0:T(8,128)(2,1)}), bf16[64,1024]{1,0:T(8,128)(2,1)}) %reduce-scatter.3.cloned.1.call-update) | async-done | bytes 131088 | tf_op jit(solution)/shard_map/reduce_scatter | solution.py:119
  195.9 1.0 fusion.73
  196.9 1.1 multiply_reduce_fusion.1
  198.0 1.7 divide_convert_fusion.3
  200.0 0.3 copy.72
  200.3 0.5 reshape_reshape.19
  200.8 23.7 %all-gather.8.cloned.1.call-done = bf16[512,1024]{1,0:T(8,128)(2,1)} async-done(((bf16[64,1024]{1,0:T(8,128)(2,1)}), bf16[512,1024]{1,0:T(8,128)(2,1)}) %all-gather.8.cloned.1.call-update) | async-done | bytes 1048592 | tf_op jit(solution)/shard_map/all_gather | solution.py:124
  224.5 5.6 %convolution_convert_fusion.1 = bf16[512,1024]{1,0:T(8,128)(2,1)} fusion(bf16[512,1024]{0,1:T(8,128)(2,1)S(1)} %bitcast.137, bf16[512,1024]{1,0:T(8,128)(2,1)} %all-gather.8.cloned.1.call-done, bf16[1024,512]{1,0:T(8,128)(2,1)S(1)} %reshape_reshape.19), kind=kOutput, calls=%fused_computation.19 | convolution fusion | flops 1091305472 | bytes 4194304 | tf_op jit(solution)/shard_map/dot_general | solution.py:127
  230.4 1.1 gather_fusion
  232.0 1.0 scatter_custom_fusion
  233.0 0.7 all_to_all.16
  233.7 10.1 %all-to-all-start = ((s32[32,1,8]{2,1,0:T(1,128)}), s32[32,1,8]{2,1,0:T(1,128)S(1)}, u32[]{:S(2)}, u32[]{:S(2)}) async-start(s32[32,1,8]{2,1,0:T(1,128)} %bitcast.36), calls=%async_computation.2 | async-start | bytes 32768 | tf_op jit(solution)/shard_map/all_to_all | solution.py:61
  243.8 0.8 slice.49
  244.6 9.9 %all_gather.19 = bf16[8,32,4,128]{3,2,0,1:T(4,128)(2,1)S(1)} all-gather(bf16[1,32,4,128]{3,2,0,1:T(4,128)(2,1)S(1)} %bitcast.145), channel_id=1, replica_groups=mesh['dp'=32,'mp'=8] {'mp'}, dimensions={0}, use_global_device_ids=true | all-gather | bytes 294912 | tf_op jit(solution)/shard_map/all_gather | solution.py:85
  254.5 11.1 %reduce-scatter.5.cloned.1.call-done = bf16[64,1024]{1,0:T(8,128)(2,1)} async-done(((bf16[512,1024]{1,0:T(8,128)(2,1)}), bf16[64,1024]{1,0:T(8,128)(2,1)}) %reduce-scatter.5.cloned.1.call-update) | async-done | bytes 131088 | tf_op jit(solution)/shard_map/reduce_scatter | solution.py:128
  265.6 1.0 fusion.71
  266.6 1.1 multiply_reduce_fusion
  267.7 1.3 multiply_reduce_fusion.2
  269.1 1.0 broadcast_in_dim.21
  270.1 10.0 %all-to-all-start.1 = ((bf16[32,2,32,128]{3,2,1,0:T(8,128)(2,1)}), bf16[32,2,32,128]{3,2,1,0:T(8,128)(2,1)S(1)}, u32[]{:S(2)}, u32[]{:S(2)}) async-start(bf16[32,2,32,128]{3,2,1,0:T(8,128)(2,1)} %broadcast_in_dim.21), calls=%async_computation.3 | async-start | bytes 1048576 | tf_op jit(solution)/shard_map/all_to_all | solution.py:139
  280.3 11.8 %gather_fusion.2 = bf16[256,128,128]{2,1,0:T(8,128)(2,1)} fusion(bf16[256,128,128]{2,1,0:T(8,128)(2,1)} %param.24, s32[1024]{0:T(1024)S(1)} %pad_clamp_fusion.1), kind=kCustom, calls=%fused_computation.2 | custom fusion | bytes 16778240 | tf_op jit(solution)/shard_map/gather | solution.py:64
  292.2 1.9 gather_fusion.1
  294.3 1.3 gather_fusion.4
  295.7 8.0 %select_reduce_fusion = bf16[32,8,32]{2,1,0:T(8,128)(2,1)S(1)} fusion(bf16[32,8,128,128]{3,2,1,0:T(8,128)(2,1)} %bitcast.134, bf16[32,8,32,128]{3,2,1,0:T(8,128)(2,1)S(1)} %bitcast.136, pred[32,8]{1,0:T(8,128)(4,1)S(1)} %compare_and_fusion, pred[32,8,128]{2,1,0:T(8,128)(4,1)S(1)} %iota_compare_fusion.1), kind=kOutput, calls=%fused_computation.8 | convolution fusion | flops 271572992 | bytes 10535168 | tf_op jit(solution)/shard_map/snie,snte->snit/dot_general | solution.py:142
  303.7 0.7 reshape.452
  304.4 9.8 %all-to-all-start.2 = ((bf16[32,2,128]{2,1,0:T(2,128)(2,1)}), bf16[32,2,128]{2,1,0:T(2,128)(2,1)S(1)}, u32[]{:S(2)}, u32[]{:S(2)}) async-start(bf16[32,2,128]{2,1,0:T(2,128)(2,1)} %reshape.452), calls=%async_computation.4 | async-start | bytes 32768 | tf_op jit(solution)/shard_map/all_to_all | solution.py:21
  314.2 8.6 %all-to-all-done.2 = bf16[32,2,128]{2,1,0:T(2,128)(2,1)S(1)} async-done(((bf16[32,2,128]{2,1,0:T(2,128)(2,1)}), bf16[32,2,128]{2,1,0:T(2,128)(2,1)S(1)}, u32[]{:S(2)}, u32[]{:S(2)}) %all-to-all-start.2) | async-done | bytes 16416 | tf_op jit(solution)/shard_map/all_to_all | solution.py:21
  322.9 0.6 gather_fusion.3
  323.6 0.7 reduce_sum.82
  (76 shorter events, 3.0 us)
Async XLA Ops:
  7.2 223.2 %copy-start = (s32[8192]{0:T(1024)S(1)}, s32[8192]{0:T(1024)}, u32[]{:S(2)}) copy-start(s32[8192]{0:T(1024)} %param.26) | copy-start | bytes 98308
  7.2 106.8 %all-gather.10.cloned.1.call-start = ((), (), s32[]{:S(2)}) async-start(), calls=%async_computation.9 | async-start | bytes 8718336 | tf_op jit(solution)/shard_map/all_gather | solution.py:70
  13.9 126.0 %all-gather.6.cloned.1.call-start = ((), (), s32[]{:S(2)}) async-start(), calls=%async_computation.5 | async-start | bytes 1179648 | tf_op jit(solution)/shard_map/all_gather | solution.py:89
  14.7 181.2 %reduce-scatter.3.cloned.1.call-start = ((), (), s32[]{:S(2)}) async-start(), calls=%async_computation.6 | async-start | bytes 1179648 | tf_op jit(solution)/shard_map/reduce_scatter | solution.py:119
  117.8 2.3 copy-start.2
  139.9 4.1 %copy-start.10 = (bf16[512,128]{0,1:T(8,128)(2,1)S(1)}, bf16[512,128]{0,1:T(8,128)(2,1)}, u32[]{:S(2)}) copy-start(bf16[512,128]{0,1:T(8,128)(2,1)} %convolution_convert_fusion.3) | copy-start | bytes 393220
  143.5 1.1 copy-start.11
  144.0 2.7 copy-start.4
  144.1 2.7 copy-start.9
  149.4 5.8 %copy-start.3 = (bf16[16,32,1024]{2,1,0:T(8,128)(2,1)S(1)}, bf16[16,32,1024]{2,1,0:T(8,128)(2,1)}, u32[]{:S(2)}) copy-start(bf16[16,32,1024]{2,1,0:T(8,128)(2,1)} %all-gather.6.cloned.1.call-done) | copy-start | bytes 3145732
  153.4 0.8 copy-start.8
  156.4 3.2 copy-start.7
  159.2 36.7 %copy-start.5 = (bf16[2,32,1024]{2,1,0:T(8,128)(2,1)S(1)}, bf16[2,32,1024]{2,1,0:T(8,128)(2,1)}, u32[]{:S(2)}) copy-start(bf16[2,32,1024]{2,1,0:T(8,128)(2,1)} %param.14) | copy-start | bytes 393220
  161.1 63.5 %all-gather.8.cloned.1.call-start = ((), (), s32[]{:S(2)}) async-start(), calls=%async_computation.7 | async-start | bytes 1179648 | tf_op jit(solution)/shard_map/all_gather | solution.py:124
  199.7 65.8 %reduce-scatter.5.cloned.1.call-start = ((), (), s32[]{:S(2)}) async-start(), calls=%async_computation.8 | async-start | bytes 1179648 | tf_op jit(solution)/shard_map/reduce_scatter | solution.py:128
  224.5 5.6 %copy-start.13 = (s32[2,16,4]{1,2,0:T(4,128)S(1)}, s32[2,16,4]{1,2,0:T(4,128)}, u32[]{:S(2)}) copy-start(s32[2,16,4]{1,2,0:T(4,128)} %param.27) | copy-start | bytes 1540
  230.1 35.4 %copy-start.6 = (bf16[64,1024]{1,0:T(8,128)(2,1)S(1)}, bf16[64,1024]{1,0:T(8,128)(2,1)}, u32[]{:S(2)}) copy-start(bf16[64,1024]{1,0:T(8,128)(2,1)} %divide_convert_fusion.3) | copy-start | bytes 393220
  233.7 35.4 %all-to-all-start = ((s32[32,1,8]{2,1,0:T(1,128)}), s32[32,1,8]{2,1,0:T(1,128)S(1)}, u32[]{:S(2)}, u32[]{:S(2)}) async-start(s32[32,1,8]{2,1,0:T(1,128)} %bitcast.36), calls=%async_computation.2 | async-start | bytes 32768 | tf_op jit(solution)/shard_map/all_to_all | solution.py:61
  269.1 23.1 %copy-start.12 = (bf16[64,128]{1,0:T(8,128)(2,1)}, bf16[64,128]{1,0:T(8,128)(2,1)S(1)}, u32[]{:S(2)}) copy-start(bf16[64,128]{1,0:T(8,128)(2,1)S(1)} %divide_convert_fusion.5) | copy-start | bytes 49156
  270.1 24.2 %all-to-all-start.1 = ((bf16[32,2,32,128]{3,2,1,0:T(8,128)(2,1)}), bf16[32,2,32,128]{3,2,1,0:T(8,128)(2,1)S(1)}, u32[]{:S(2)}, u32[]{:S(2)}) async-start(bf16[32,2,32,128]{3,2,1,0:T(8,128)(2,1)} %broadcast_in_dim.21), calls=%async_computation.3 | async-start | bytes 1048576 | tf_op jit(solution)/shard_map/all_to_all | solution.py:139
  280.3 11.9 %copy-start.1 = (s32[256]{0:T(256)S(1)}, s32[256]{0:T(256)}, u32[]{:S(2)}) copy-start(s32[256]{0:T(256)} %param.25) | copy-start | bytes 3076
  304.4 18.4 %all-to-all-start.2 = ((bf16[32,2,128]{2,1,0:T(2,128)(2,1)}), bf16[32,2,128]{2,1,0:T(2,128)(2,1)S(1)}, u32[]{:S(2)}, u32[]{:S(2)}) async-start(bf16[32,2,128]{2,1,0:T(2,128)(2,1)} %reshape.452), calls=%async_computation.4 | async-start | bytes 32768 | tf_op jit(solution)/shard_map/all_to_all | solution.py:21
Sparse Core Ops, SparseCore 0:
  14.0 99.8 all-gather.9
  115.8 24.0 all-gather.5
  161.2 34.6 reduce-scatter.2
  199.9 24.6 all-gather.7
  230.3 35.2 reduce-scatter.4
where the time goes:
time: 332 us; the launch traced here: 331 us
  waiting for transfers between devices  190 us (57%)
  local copies, waits for them, and re-layouts  45.7 us (14%)
  matrix products  32.7 us (10%)
  starting transfers between devices  30.3 us (9%)
  between operations  14.3 us (4%)
  blocking collectives  9.85 us (3%)
  other arithmetic  7.6 us (2%)
    all_gather x1, waiting for transfers between devices, body(): gathered = lax.all_gather(flat_pieces, 'dp', axis=0, tiled=False)  99.2 us
    reduce_scatter x1, waiting for transfers between devices, body(): lax.psum_scatter(attn_terms.astype(jnp.bfloat16), 'mp', scatter_dimension...  34.7 us
    all_gather x1, waiting for transfers between devices, body(): mid_all = lax.all_gather(mid, 'mp', axis=0, tiled=True)  23.7 us
    unnamed x46, local copies, waits for them, and re-layouts  13.4 us
    all_gather x1, waiting for transfers between devices, body(): tokens = lax.all_gather(hidden, 'mp', axis=0, tiled=True)  12.2 us
    gather x1, local copies, waits for them, and re-layouts, body(): chosen = pages[where_local]  11.8 us
    reduce_scatter x1, waiting for transfers between devices, body(): lax.psum_scatter(down_terms.astype(jnp.bfloat16), 'mp', scatter_dimension...  11.1 us
    all_to_all x1, starting transfers between devices, body(): got = lax.all_to_all(codes, 'dp', split_axis=0, concat_axis=0, tiled=True)  10.1 us
  transfers between devices with their start and end apart: 8, of which 6 were waited for; matrix products, arithmetic and copies ran while one was open for 11% of the time, Pallas kernels for 0%

commit v1 on v0

--- a/solution.py
+++ b/solution.py
@@ -86,7 +86,9 @@
     wp = jnp.transpose(proj_all, (1, 0, 2, 3)).reshape(
         page_owners * n_mp * w_proj.shape[0], w_proj.shape[1]
     )
-    tokens = lax.all_gather(hidden, "mp", axis=0, tiled=True)
+    tokens = jnp.concatenate(
+        lax.all_to_all(jnp.stack([hidden] * lax.axis_size("mp")), "mp", 0, 0), axis=0
+    )
     group = tokens.shape[0]
     flat = tokens.reshape(group * qlen, width)
     qsum = add_rows(flat, wq)

time: 332 us -> 312 us (0.940)
  waiting for transfers between devices: 190 us -> 170 us
  starting transfers between devices: 30.3 us -> 34.5 us
    all_gather x1 -> x0, waiting for transfers between devices: 12.2 us -> none  [body(): tokens = lax.all_gather(hidden, 'mp', axis=0, tiled=True)]
    all_gather x1, waiting for transfers between devices: 99.2 us -> 93.6 us  [body(): gathered = lax.all_gather(flat_pieces, 'dp', axis=0, tiled=False)]
    all_to_all x0 -> x1, starting transfers between devices: none -> 4.3 us  [body(): lax.all_to_all(jnp.stack([hidden] * lax.axis_size('mp')), 'mp', 0, 0)]
  transfers between devices with their start and end apart: 8 -> 8, of which waited for: 6 -> 5; matrix products, arithmetic and copies ran while one was open for 11% -> 12% of each run, Pallas kernels for 0% -> 0%
where the time goes in v1:
time: 312 us; the launch traced here: 311 us
  waiting for transfers between devices  170 us (54%)
  local copies, waits for them, and re-layouts  44.9 us (14%)
  starting transfers between devices  34.5 us (11%)
  matrix products  29.7 us (10%)
  between operations  14.3 us (5%)
  blocking collectives  9.85 us (3%)
  other arithmetic  7.6 us (2%)
    all_gather x1, waiting for transfers between devices, body(): gathered = lax.all_gather(flat_pieces, 'dp', axis=0, tiled=False)  93.6 us
    reduce_scatter x1, waiting for transfers between devices, body(): lax.psum_scatter(attn_terms.astype(jnp.bfloat16), 'mp', scatter_dimension...  33.1 us
    all_gather x1, waiting for transfers between devices, body(): mid_all = lax.all_gather(mid, 'mp', axis=0, tiled=True)  23.7 us
    unnamed x46, local copies, waits for them, and re-layouts  13.3 us
    gather x1, local copies, waits for them, and re-layouts, body(): chosen = pages[where_local]  11.8 us
    reduce_scatter x1, waiting for transfers between devices, body(): lax.psum_scatter(down_terms.astype(jnp.bfloat16), 'mp', scatter_dimension...  11.1 us
    all_to_all x1, starting transfers between devices, body(): got = lax.all_to_all(codes, 'dp', split_axis=0, concat_axis=0, tiled=True)  10.1 us
    all_to_all x1, starting transfers between devices, body(): recv = lax.all_to_all(sent, 'dp', split_axis=0, concat_axis=0, tiled=True)  9.96 us
  transfers between devices with their start and end apart: 8, of which 5 were waited for; matrix products, arithmetic and copies ran while one was open for 12% of the time, Pallas kernels for 0%

profile of v1, /device:TPU:8, one launch (start us, length us, event | category | flops | bytes accessed | tf_op | source)
XLA Modules:
  0.0 311.2 jit_solution(2329518231415601937)
XLA Ops:
  7.2 0.7 bitcast_dynamic-update-slice_fusion.3
  7.9 0.8 copy.68
  8.7 0.8 copy.69
  9.5 0.8 copy.70
  10.2 0.7 bitcast_dynamic-update-slice_fusion.2
  10.9 0.7 bitcast_dynamic-update-slice_fusion.1
  11.6 0.7 bitcast_dynamic-update-slice_fusion
  12.4 0.7 constant_dynamic-update-slice_fusion
  13.0 0.8 reshape.442
  13.9 2.1 stack.2
  16.0 4.3 %all-to-all-start = ((bf16[8,2,32,1024]{3,2,1,0:T(8,128)(2,1)}), bf16[8,2,32,1024]{3,2,1,0:T(8,128)(2,1)S(1)}, u32[]{:S(2)}, u32[]{:S(2)}) async-start(bf16[8,2,32,1024]{3,2,1,0:T(8,128)(2,1)} %stack.2), calls=%async_computation | async-start | bytes 2097152 | tf_op jit(solution)/shard_map/all_to_all | solution.py:90
  20.3 93.6 %all-gather.7.cloned.1.call-done = bf16[32,1,66048]{2,1,0:T(2,128)(2,1)} async-done(((bf16[1,1,66048]{2,1,0:T(2,128)(2,1)}), bf16[32,1,66048]{2,1,0:T(2,128)(2,1)}) %all-gather.7.cloned.1.call-update) | async-done | bytes 4227088 | tf_op jit(solution)/shard_map/all_gather | solution.py:70
  113.9 3.9 %copy.85 = bf16[32,1,66048]{2,0,1:T(8,128)(2,1)S(1)} copy(bf16[32,1,66048]{2,1,0:T(2,128)(2,1)} %all-gather.7.cloned.1.call-done) | data formatting | bytes 8454144
  117.8 1.9 fusion.123
  119.7 0.8 copy-done.2
  120.4 0.9 slice_bitcast_fusion
  121.5 1.6 reshape_reshape.22
  123.0 1.8 reshape_reshape.21
  124.8 1.2 convolution_convert_fusion.3
  126.0 2.1 convolution_convert_fusion.4
  128.0 1.5 fusion.17
  129.5 0.5 fusion.16
  130.6 0.5 fusion.63
  131.1 2.2 fusion.1
  133.3 0.5 fusion.65
  133.8 1.4 fusion.3
  135.2 1.1 copy.56
  136.3 1.6 fusion.13
  137.9 0.2 fusion.124
  138.3 0.5 copy-done.8
  138.7 0.5 fusion.15
  139.5 1.5 fusion.14
  141.1 0.2 copy.61
  141.5 1.4 convolution_convert_fusion
  143.1 33.1 %reduce-scatter.3.cloned.1.call-done = bf16[64,1024]{1,0:T(8,128)(2,1)} async-done(((bf16[512,1024]{1,0:T(8,128)(2,1)}), bf16[64,1024]{1,0:T(8,128)(2,1)}) %reduce-scatter.3.cloned.1.call-update) | async-done | bytes 131088 | tf_op jit(solution)/shard_map/reduce_scatter | solution.py:121
  176.2 1.0 fusion.73
  177.3 1.1 multiply_reduce_fusion.1
  178.4 1.7 divide_convert_fusion.3
  180.1 0.2 reduce-scatter.5.cloned.1.call-start
  180.3 0.3 copy.72
  180.7 0.5 reshape_reshape.23
  181.2 23.7 %all-gather.5.cloned.1.call-done = bf16[512,1024]{1,0:T(8,128)(2,1)} async-done(((bf16[64,1024]{1,0:T(8,128)(2,1)}), bf16[512,1024]{1,0:T(8,128)(2,1)}) %all-gather.5.cloned.1.call-update) | async-done | bytes 1048592 | tf_op jit(solution)/shard_map/all_gather | solution.py:126
  204.9 5.6 %convolution_convert_fusion.1 = bf16[512,1024]{1,0:T(8,128)(2,1)} fusion(bf16[512,1024]{0,1:T(8,128)(2,1)S(1)} %bitcast.137, bf16[512,1024]{1,0:T(8,128)(2,1)} %all-gather.5.cloned.1.call-done, bf16[1024,512]{1,0:T(8,128)(2,1)S(1)} %reshape_reshape.23), kind=kOutput, calls=%fused_computation.19 | convolution fusion | flops 1091305472 | bytes 4194304 | tf_op jit(solution)/shard_map/dot_general | solution.py:129
  210.8 1.1 gather_fusion
  212.4 1.0 scatter_custom_fusion
  213.4 0.7 all_to_all.20
  214.1 10.1 %all-to-all-start.1 = ((s32[32,1,8]{2,1,0:T(1,128)}), s32[32,1,8]{2,1,0:T(1,128)S(1)}, u32[]{:S(2)}, u32[]{:S(2)}) async-start(s32[32,1,8]{2,1,0:T(1,128)} %bitcast.36), calls=%async_computation.3 | async-start | bytes 32768 | tf_op jit(solution)/shard_map/all_to_all | solution.py:61
  224.2 0.8 slice.49
  225.0 9.9 %all_gather.15 = bf16[8,32,4,128]{3,2,0,1:T(4,128)(2,1)S(1)} all-gather(bf16[1,32,4,128]{3,2,0,1:T(4,128)(2,1)S(1)} %bitcast.145), channel_id=1, replica_groups=mesh['dp'=32,'mp'=8] {'mp'}, dimensions={0}, use_global_device_ids=true | all-gather | bytes 294912 | tf_op jit(solution)/shard_map/all_gather | solution.py:85
  234.8 11.1 %reduce-scatter.5.cloned.1.call-done = bf16[64,1024]{1,0:T(8,128)(2,1)} async-done(((bf16[512,1024]{1,0:T(8,128)(2,1)}), bf16[64,1024]{1,0:T(8,128)(2,1)}) %reduce-scatter.5.cloned.1.call-update) | async-done | bytes 131088 | tf_op jit(solution)/shard_map/reduce_scatter | solution.py:130
  245.9 1.0 fusion.71
  247.0 1.1 multiply_reduce_fusion
  248.1 1.3 multiply_reduce_fusion.2
  249.5 1.0 broadcast_in_dim.21
  250.5 10.0 %all-to-all-start.2 = ((bf16[32,2,32,128]{3,2,1,0:T(8,128)(2,1)}), bf16[32,2,32,128]{3,2,1,0:T(8,128)(2,1)S(1)}, u32[]{:S(2)}, u32[]{:S(2)}) async-start(bf16[32,2,32,128]{3,2,1,0:T(8,128)(2,1)} %broadcast_in_dim.21), calls=%async_computation.4 | async-start | bytes 1048576 | tf_op jit(solution)/shard_map/all_to_all | solution.py:141
  260.7 11.8 %gather_fusion.2 = bf16[256,128,128]{2,1,0:T(8,128)(2,1)} fusion(bf16[256,128,128]{2,1,0:T(8,128)(2,1)} %param.24, s32[1024]{0:T(1024)S(1)} %pad_clamp_fusion.1), kind=kCustom, calls=%fused_computation.2 | custom fusion | bytes 16778240 | tf_op jit(solution)/shard_map/gather | solution.py:64
  272.5 1.9 gather_fusion.1
  274.7 1.3 gather_fusion.4
  276.0 8.0 %select_reduce_fusion = bf16[32,8,32]{2,1,0:T(8,128)(2,1)S(1)} fusion(bf16[32,8,128,128]{3,2,1,0:T(8,128)(2,1)} %bitcast.134, bf16[32,8,32,128]{3,2,1,0:T(8,128)(2,1)S(1)} %bitcast.136, pred[32,8]{1,0:T(8,128)(4,1)S(1)} %compare_and_fusion, pred[32,8,128]{2,1,0:T(8,128)(4,1)S(1)} %iota_compare_fusion.1), kind=kOutput, calls=%fused_computation.8 | convolution fusion | flops 271572992 | bytes 10535168 | tf_op jit(solution)/shard_map/snie,snte->snit/dot_general | solution.py:144
  284.1 0.7 reshape.450
  284.8 9.8 %all-to-all-start.3 = ((bf16[32,2,128]{2,1,0:T(2,128)(2,1)}), bf16[32,2,128]{2,1,0:T(2,128)(2,1)S(1)}, u32[]{:S(2)}, u32[]{:S(2)}) async-start(bf16[32,2,128]{2,1,0:T(2,128)(2,1)} %reshape.450), calls=%async_computation.5 | async-start | bytes 32768 | tf_op jit(solution)/shard_map/all_to_all | solution.py:21
  294.6 8.6 %all-to-all-done.3 = bf16[32,2,128]{2,1,0:T(2,128)(2,1)S(1)} async-done(((bf16[32,2,128]{2,1,0:T(2,128)(2,1)}), bf16[32,2,128]{2,1,0:T(2,128)(2,1)S(1)}, u32[]{:S(2)}, u32[]{:S(2)}) %all-to-all-start.3) | async-done | bytes 16416 | tf_op jit(solution)/shard_map/all_to_all | solution.py:21
  303.3 0.6 gather_fusion.3
  304.0 0.7 reduce_sum.82
  (76 shorter events, 2.8 us)
Async XLA Ops:
  7.2 203.6 %copy-start = (s32[8192]{0:T(1024)S(1)}, s32[8192]{0:T(1024)}, u32[]{:S(2)}) copy-start(s32[8192]{0:T(1024)} %param.26) | copy-start | bytes 98308
  7.2 106.8 %all-gather.7.cloned.1.call-start = ((), (), s32[]{:S(2)}) async-start(), calls=%async_computation.9 | async-start | bytes 8718336 | tf_op jit(solution)/shard_map/all_gather | solution.py:70
  16.0 112.1 %all-to-all-start = ((bf16[8,2,32,1024]{3,2,1,0:T(8,128)(2,1)}), bf16[8,2,32,1024]{3,2,1,0:T(8,128)(2,1)S(1)}, u32[]{:S(2)}, u32[]{:S(2)}) async-start(bf16[8,2,32,1024]{3,2,1,0:T(8,128)(2,1)} %stack.2), calls=%async_computation | async-start | bytes 2097152 | tf_op jit(solution)/shard_map/all_to_all | solution.py:90
  20.3 155.9 %reduce-scatter.3.cloned.1.call-start = ((), (), s32[]{:S(2)}) async-start(), calls=%async_computation.6 | async-start | bytes 1179648 | tf_op jit(solution)/shard_map/reduce_scatter | solution.py:121
  117.8 2.6 copy-start.2
  128.0 2.5 copy-start.10
  130.0 1.1 copy-start.11
  130.6 2.7 copy-start.9
  135.2 3.0 copy-start.7
  137.9 0.8 copy-start.8
  139.2 2.2 copy-start.6
  141.1 35.2 %copy-start.4 = (bf16[2,32,1024]{2,1,0:T(8,128)(2,1)S(1)}, bf16[2,32,1024]{2,1,0:T(8,128)(2,1)}, u32[]{:S(2)}) copy-start(bf16[2,32,1024]{2,1,0:T(8,128)(2,1)} %param.14) | copy-start | bytes 393220
  141.5 38.8 %copy-start.3 = (bf16[32,16384]{1,0:T(8,128)(2,1)S(1)}, bf16[32,16384]{1,0:T(8,128)(2,1)}, u32[]{:S(2)}) copy-start(bf16[32,16384]{1,0:T(8,128)(2,1)} %get-tuple-element.3) | copy-start | bytes 3145732
  143.0 61.9 %all-gather.5.cloned.1.call-start = ((), (), s32[]{:S(2)}) async-start(), calls=%async_computation.7 | async-start | bytes 1179648 | tf_op jit(solution)/shard_map/all_gather | solution.py:126
  180.1 65.8 %reduce-scatter.5.cloned.1.call-start = ((), (), s32[]{:S(2)}) async-start(), calls=%async_computation.8 | async-start | bytes 1179648 | tf_op jit(solution)/shard_map/reduce_scatter | solution.py:130
  204.9 5.6 %copy-start.13 = (s32[2,16,4]{1,2,0:T(4,128)S(1)}, s32[2,16,4]{1,2,0:T(4,128)}, u32[]{:S(2)}) copy-start(s32[2,16,4]{1,2,0:T(4,128)} %param.27) | copy-start | bytes 1540
  210.5 35.4 %copy-start.5 = (bf16[64,1024]{1,0:T(8,128)(2,1)S(1)}, bf16[64,1024]{1,0:T(8,128)(2,1)}, u32[]{:S(2)}) copy-start(bf16[64,1024]{1,0:T(8,128)(2,1)} %divide_convert_fusion.3) | copy-start | bytes 393220
  214.1 35.4 %all-to-all-start.1 = ((s32[32,1,8]{2,1,0:T(1,128)}), s32[32,1,8]{2,1,0:T(1,128)S(1)}, u32[]{:S(2)}, u32[]{:S(2)}) async-start(s32[32,1,8]{2,1,0:T(1,128)} %bitcast.36), calls=%async_computation.3 | async-start | bytes 32768 | tf_op jit(solution)/shard_map/all_to_all | solution.py:61
  249.5 23.0 %copy-start.12 = (bf16[64,128]{1,0:T(8,128)(2,1)}, bf16[64,128]{1,0:T(8,128)(2,1)S(1)}, u32[]{:S(2)}) copy-start(bf16[64,128]{1,0:T(8,128)(2,1)S(1)} %divide_convert_fusion.5) | copy-start | bytes 49156
  250.5 24.2 %all-to-all-start.2 = ((bf16[32,2,32,128]{3,2,1,0:T(8,128)(2,1)}), bf16[32,2,32,128]{3,2,1,0:T(8,128)(2,1)S(1)}, u32[]{:S(2)}, u32[]{:S(2)}) async-start(bf16[32,2,32,128]{3,2,1,0:T(8,128)(2,1)} %broadcast_in_dim.21), calls=%async_computation.4 | async-start | bytes 1048576 | tf_op jit(solution)/shard_map/all_to_all | solution.py:141
  260.7 11.9 %copy-start.1 = (s32[256]{0:T(256)S(1)}, s32[256]{0:T(256)}, u32[]{:S(2)}) copy-start(s32[256]{0:T(256)} %param.25) | copy-start | bytes 3076
  284.8 18.4 %all-to-all-start.3 = ((bf16[32,2,128]{2,1,0:T(2,128)(2,1)}), bf16[32,2,128]{2,1,0:T(2,128)(2,1)S(1)}, u32[]{:S(2)}, u32[]{:S(2)}) async-start(bf16[32,2,128]{2,1,0:T(2,128)(2,1)} %reshape.450), calls=%async_computation.5 | async-start | bytes 32768 | tf_op jit(solution)/shard_map/all_to_all | solution.py:21
Sparse Core Ops, SparseCore 0:
  14.0 99.8 all-gather.6
  143.1 33.0 reduce-scatter.2
  180.2 24.6 all-gather.4
  210.6 35.2 reduce-scatter.4
